TPU v7x, 512 devices: a whole 4x8x8 slice. The times are simulated.
512 devices in a mesh: wide: 64 (over z, x, core), narrow: 8 (over y).
Axes of the slice: x: 4, y: 8, z: 8, core: 2. Of those that a mesh axis runs over, the one named last changes fastest.
Arguments:
- hidden_in: bfloat16 [16384, 2048], P('wide', 'narrow'), may hold values from -6 to 6
- segment_ids: int32 [16384], P('wide'), may hold values from 0 to 31, never falling along the last dimension, each value on 1 to 2048 neighbouring positions
- page_table: int32 [1024], P('wide'), may hold values from 0 to 1023, as said below
- wq: bfloat16 [2048, 2048], P('wide', 'narrow')
- wk: bfloat16 [2048, 2048], P('wide', 'narrow')
- wv: bfloat16 [2048, 2048], P('wide', 'narrow'), may hold values from -0.125 to 0.125
- wo: bfloat16 [2048, 2048], P('narrow', 'wide'), may hold values from -0.125 to 0.125
- wg: bfloat16 [2048, 4096], P('wide', 'narrow'), may hold values from -0.125 to 0.125
- wu: bfloat16 [2048, 4096], P('wide', 'narrow'), may hold values from -0.125 to 0.125
- wd: bfloat16 [4096, 2048], P('narrow', 'wide'), may hold values from -0.09375 to 0.09375
Outputs:
- result: bfloat16 [16384, 2048], P('wide', 'narrow')
- kv_cache: bfloat16 [2, 1024, 16, 2048], P(None, 'wide', None, 'narrow')
Inputs may be any that keep to these rules, and one draw needn't show every extreme that they name: `page_table`: entries 16 * w to 16 * (w + 1) - 1 of the table are a permutation of those same numbers, for every w.
All inputs are finite; a program needn't handle non-finite values.
Results may differ from a plain program's by a relative error of at most 0.017.
Values may be sent and summed in bfloat16 or wider, within the bound.
No kernel may reach another device: no remote copies, remote signals or barrier semaphores. Data moves between devices by JAX's collectives and lax.ppermute only.
A program may use at most 64 MiB of HBM per device.

v0:
```python
import jax
import jax.numpy as jnp
from jax import lax
from jax.sharding import PartitionSpec as P

HEAD_DIM = 128
REACH = 8
PAGE = 16
epsilon = 1e-05
rope_base = 10000.0


def prefix(value, axis, join, neutral):
    count, mine = (lax.axis_size(axis), lax.axis_index(axis))
    pieces = jax.tree.map(lambda part: lax.all_gather(part, axis), value)
    running = jax.tree.map(
        lambda part, zero: jnp.full_like(part, 0) + jnp.asarray(zero, part.dtype), value, neutral
    )

    def lap(position, running):
        longer = join(running, jax.tree.map(lambda part: part[position], pieces))
        return jax.tree.map(lambda new, old: jnp.where(position < mine, new, old), longer, running)

    return lax.fori_loop(0, count - 1, lap, running)


def shifted(value, axis, steps):
    count = lax.axis_size(axis)
    first, last = (max(0, -steps), min(count, count - steps))
    return lax.ppermute(value, axis, [(source, source + steps) for source in range(first, last)])


def norm_rows(source):
    widened = source.astype(jnp.float32)
    center = widened - jnp.mean(widened, axis=-1, keepdims=True)
    spread = jnp.mean(center * center, axis=-1, keepdims=True)
    return (center * lax.rsqrt(spread + epsilon)).astype(jnp.bfloat16)


def rotate(projected, positions):
    head_size = projected.shape[-1]
    half_dim = head_size // 2
    frequency = jnp.power(rope_base, -jnp.arange(half_dim, dtype=jnp.float32) * 2.0 / head_size)
    angles = positions.astype(jnp.float32)[:, None] * frequency[None, :]
    cosine = jnp.cos(angles)[:, None, :]
    sine_part = jnp.sin(angles)[:, None, :]
    first_half = projected[..., :half_dim]
    second_half = projected[..., half_dim:]
    return jnp.concatenate(
        [
            first_half * cosine - second_half * sine_part,
            second_half * cosine + first_half * sine_part,
        ],
        axis=-1,
    )


def join_runs(earlier, later):
    early_last, early_trailing, early_single = earlier
    late_last, late_trailing, late_single = later
    late_empty = late_trailing == 0
    same_id = (early_last == late_last).astype(jnp.int32)
    linked = (late_single == 1) & (same_id == 1) & (early_trailing > 0)
    last_id = jnp.where(late_empty, early_last, late_last)
    trailing = jnp.where(
        late_empty, early_trailing, late_trailing + jnp.where(linked, early_trailing, 0)
    )
    single = jnp.where(
        late_empty,
        early_single,
        jnp.where(early_trailing == 0, late_single, late_single * early_single * same_id),
    )
    return (last_id, trailing, single)


def add_rows(source, piece):
    return jnp.dot(source, piece, preferred_element_type=jnp.float32)


def per_device(hidden_in, segment_ids, page_table, wq, wk, wv, wo, wg, wu, wd):
    tok_rows = hidden_in.shape[0]
    wide_rank = lax.axis_index("wide")
    local_index = jnp.arange(tok_rows, dtype=jnp.int32)
    run_last = segment_ids[tok_rows - 1]
    run_trailing = jnp.sum((segment_ids == run_last).astype(jnp.int32))
    run_single = (segment_ids[0] == run_last).astype(jnp.int32)
    earlier = prefix(
        (run_last, run_trailing, run_single),
        "wide",
        join_runs,
        (jnp.int32(-1), jnp.int32(0), jnp.int32(1)),
    )
    lower_count = jnp.sum((segment_ids[None, :] < segment_ids[:, None]).astype(jnp.int32), axis=1)
    carried = jnp.where(
        (segment_ids == earlier[0]) & (segment_ids == segment_ids[0]), earlier[1], 0
    )
    positions = local_index - lower_count + carried
    global_index = wide_rank * tok_rows + local_index
    query_start = global_index - positions
    whole = lax.all_gather(hidden_in, "narrow", axis=1, tiled=True)
    normed = norm_rows(whole)
    local_width = wq.shape[1]
    head_count = local_width // HEAD_DIM

    def add_normed(piece):
        return add_rows(normed, piece)

    q_proj = add_normed(lax.all_gather(wq, "wide", axis=0, tiled=True))
    k_proj = add_normed(lax.all_gather(wk, "wide", axis=0, tiled=True))
    v_proj = add_normed(lax.all_gather(wv, "wide", axis=0, tiled=True))
    queries = rotate(q_proj.reshape(tok_rows, head_count, HEAD_DIM), positions).astype(jnp.bfloat16)
    keys_rot = rotate(k_proj.reshape(tok_rows, head_count, HEAD_DIM), positions).astype(
        jnp.bfloat16
    )
    values = v_proj.astype(jnp.bfloat16).reshape(tok_rows, head_count, HEAD_DIM)
    current = (keys_rot, values)
    blocks = [current]
    for step_back in range(REACH):
        current = shifted((current[0], current[1]), "wide", 1)
        blocks.append(current)
    score_scale = HEAD_DIM ** (-0.5)
    ordered = blocks[::-1]
    key_all = jnp.concatenate([member[0] for member in ordered], axis=0)
    value_all = jnp.concatenate([member[1] for member in ordered], axis=0)
    key_index = (wide_rank - REACH) * tok_rows + jnp.arange((REACH + 1) * tok_rows, dtype=jnp.int32)
    allowed = (key_index[None, :] >= query_start[:, None]) & (
        key_index[None, :] <= global_index[:, None]
    )
    scores = (
        jnp.einsum("qhd,khd->hqk", queries, key_all, preferred_element_type=jnp.float32)
        * score_scale
    )
    scores = jnp.where(allowed[None], scores, -1e30)
    row_peak = jnp.max(scores, axis=-1, keepdims=True)
    exps = jnp.where(allowed[None], jnp.exp(scores - row_peak), 0.0)
    attn_probs = (exps / jnp.sum(exps, axis=-1, keepdims=True)).astype(jnp.bfloat16)
    mixed = jnp.einsum("hqk,khd->qhd", attn_probs, value_all, preferred_element_type=jnp.float32)
    attended = mixed.astype(jnp.bfloat16).reshape(tok_rows, local_width)
    attn_terms = jnp.dot(
        attended, lax.all_gather(wo, "wide", axis=1, tiled=True), preferred_element_type=jnp.float32
    )
    attn_sum = lax.psum_scatter(
        attn_terms.astype(jnp.bfloat16), "narrow", scatter_dimension=1, tiled=True
    ).astype(jnp.float32)
    first_res = (hidden_in.astype(jnp.float32) + attn_sum).astype(jnp.bfloat16)
    whole_two = lax.all_gather(first_res, "narrow", axis=1, tiled=True)
    normed_two = norm_rows(whole_two)

    def add_second(piece):
        return add_rows(normed_two, piece)

    gate_proj = add_second(lax.all_gather(wg, "wide", axis=0, tiled=True))
    up_proj = add_second(lax.all_gather(wu, "wide", axis=0, tiled=True))
    hidden = (jax.nn.silu(gate_proj) * up_proj).astype(jnp.bfloat16)
    down_terms = jnp.dot(
        hidden, lax.all_gather(wd, "wide", axis=1, tiled=True), preferred_element_type=jnp.float32
    )
    down_sum = lax.psum_scatter(
        down_terms.astype(jnp.bfloat16), "narrow", scatter_dimension=1, tiled=True
    ).astype(jnp.float32)
    result = (first_res.astype(jnp.float32) + down_sum).astype(jnp.bfloat16)
    page_count = tok_rows // PAGE
    slots = page_table - wide_rank * page_count
    pairs = jnp.stack(
        [
            keys_rot.reshape(page_count, PAGE, local_width),
            values.reshape(page_count, PAGE, local_width),
        ],
        axis=0,
    )
    kv_cache = jnp.zeros_like(pairs).at[:, slots].set(pairs)
    return (result, kv_cache)


def solution(mesh):
    return jax.shard_map(
        per_device,
        mesh=mesh,
        in_specs=(
            P("wide", "narrow"),
            P("wide"),
            P("wide"),
            P("wide", "narrow"),
            P("wide", "narrow"),
            P("wide", "narrow"),
            P("narrow", "wide"),
            P("wide", "narrow"),
            P("wide", "narrow"),
            P("narrow", "wide"),
        ),
        out_specs=(P("wide", "narrow"), P(None, "wide", None, "narrow")),
        check_vma=False,
    )
```

profile of v0, /device:TPU:2, one launch (start us, length us, event | category | flops | bytes accessed | tf_op | source)
XLA Modules:
  0.0 878.4 jit_solution(14633172779645840433)
XLA Ops:
  11.0 1.3 dynamic-slice
  12.3 2.0 fusion.47
  14.3 2.0 fusion.27
  18.3 1.4 dynamic-update-slice
  19.8 25.7 %all-reduce.3 = (s32[64]{0:T(128)S(1)}, s32[64]{0:T(128)S(1)}, s32[64]{0:T(128)S(1)}) all-reduce(s32[64]{0:T(128)S(1)} %dynamic-update-slice, s32[64]{0:T(128)S(1)} %get-tuple-element.159, s32[64]{0:T(128)S(1)} %dynamic-update-slice.2), channel_id=1, replica_groups=mesh['wide'=64,'narrow'=8] {'wide'}, use_global_device_ids=true, to_apply=%add | all-reduce | flops 192 | bytes 1536
  45.5 335.9 %while.15 = (s32[]{:T(128)}, s32[]{:T(128)}, s32[]{:T(128)}, s32[]{:T(128)}, s32[64]{0:T(128)S(1)}, /*index=5*/s32[64]{0:T(128)S(1)}, s32[64]{0:T(128)S(1)}, s32[]{:T(128)}, s32[]{:T(128)}, s32[1]{0:T(128)}) while((s32[]{:T(128)}, s32[]{:T(128)}, s32[]{:T(128)}, s32[]{:T(128)}, s32[64]{0:T(128)S(1)}, /*index=5*/s32[64]{0:T(128)S(1)}, ...), condition=%wide.region_5.6_spmd, body=%wide.region_4.5_spmd.sunk | while | flops 17 | bytes 279 | solution.py:24
  381.3 1.3 fusion.43
  383.2 1.5 convert_reduce_fusion.1
  385.6 1.7 fusion.52
  387.8 1.9 collective-permute-start.8
  389.8 1.7 convolution_convert_fusion.2
  391.6 2.5 collective-permute-start
  394.1 1.9 collective-permute-start.9
  396.1 1.8 collective-permute-done
  397.9 1.9 collective-permute-start.1
  400.4 1.9 collective-permute-start.10
  402.4 1.7 collective-permute-done.1
  404.1 1.9 collective-permute-start.2
  406.7 1.9 collective-permute-start.11
  408.6 1.8 collective-permute-done.2
  410.4 2.2 collective-permute-start.3
  413.1 3.3 collective-permute-start.12
  416.9 4.6 collective-permute-start.4
  421.6 3.6 collective-permute-start.13
  425.2 1.7 fusion.51
  427.0 4.6 collective-permute-start.5
  431.7 3.7 collective-permute-start.14
  435.7 4.7 collective-permute-start.6
  440.4 3.2 collective-permute-start.15
  444.4 5.0 collective-permute-start.7
  452.5 1.4 constant_dynamic-update-slice_fusion.5
  454.0 1.0 copy-done.8
  455.0 5.9 fusion.48
  460.9 3.7 fusion.15
  464.6 22.8 %all-gather.18.cloned.1.call-done = bf16[256,2048]{0,1:T(8,128)(2,1)} async-done(((bf16[256,32]{0,1:T(8,128)(2,1)}), bf16[256,2048]{0,1:T(8,128)(2,1)}) %all-gather.18.cloned.1.call-update) | async-done | bytes 1048592 | tf_op jit(solution)/shard_map/all_gather | solution.py:140
  487.4 2.7 convolution_convert_fusion.1
  490.2 39.1 %reduce-scatter.3.cloned.1.call-done = bf16[256,256]{1,0:T(8,128)(2,1)} async-done(((bf16[256,2048]{1,0:T(8,128)(2,1)}), bf16[256,256]{1,0:T(8,128)(2,1)}) %reduce-scatter.3.cloned.1.call-update) | async-done | bytes 131088 | tf_op jit(solution)/shard_map/reduce_scatter | solution.py:142
  529.3 1.6 add_convert_fusion.1
  533.2 40.0 %all-gather.20.cloned.1.call-done = bf16[256,2048]{1,0:T(8,128)(2,1)} async-done(((bf16[256,256]{1,0:T(8,128)(2,1)}), bf16[256,2048]{1,0:T(8,128)(2,1)}) %all-gather.20.cloned.1.call-update) | async-done | bytes 1048592 | tf_op jit(solution)/shard_map/all_gather | solution.py:146
  573.2 1.5 convert_reduce_fusion
  575.2 83.4 %all-gather.22.cloned.1.call-done = bf16[2048,512]{1,0:T(8,128)(2,1)} async-done(((bf16[32,512]{1,0:T(8,128)(2,1)}), bf16[2048,512]{1,0:T(8,128)(2,1)}) %all-gather.22.cloned.1.call-update) | async-done | bytes 2097168 | tf_op jit(solution)/shard_map/all_gather | solution.py:152
  658.6 2.3 fusion.41
  660.9 81.6 %all-gather.24.cloned.1.call-done = bf16[2048,512]{1,0:T(8,128)(2,1)} async-done(((bf16[32,512]{1,0:T(8,128)(2,1)}), bf16[2048,512]{1,0:T(8,128)(2,1)}) %all-gather.24.cloned.1.call-update) | async-done | bytes 2097168 | tf_op jit(solution)/shard_map/all_gather | solution.py:153
  742.6 83.8 %all-gather.26.cloned.1.call-done = bf16[512,2048]{0,1:T(8,128)(2,1)} async-done(((bf16[512,32]{0,1:T(8,128)(2,1)}), bf16[512,2048]{0,1:T(8,128)(2,1)}) %all-gather.26.cloned.1.call-update) | async-done | bytes 2097168 | tf_op jit(solution)/shard_map/all_gather | solution.py:156
  826.4 4.7 convolution_convert_fusion
  831.5 1.2 scatter_fusion
  832.7 37.6 %reduce-scatter.5.cloned.1.call-done = bf16[256,256]{1,0:T(8,128)(2,1)} async-done(((bf16[256,2048]{1,0:T(8,128)(2,1)}), bf16[256,256]{1,0:T(8,128)(2,1)}) %reduce-scatter.5.cloned.1.call-update) | async-done | bytes 131088 | tf_op jit(solution)/shard_map/reduce_scatter | solution.py:158
  870.3 1.6 add_convert_fusion
  (297 shorter events, 139.8 us)
Async XLA Ops:
  7.2 376.1 %all-gather.10.cloned.1.call-start = ((), (), s32[]{:S(2)}) async-start(), calls=%async_computation.2 | async-start | bytes 1179648 | tf_op jit(solution)/shard_map/all_gather | solution.py:100
  7.9 377.7 %all-gather.16.cloned.1.call-start = ((), (), s32[]{:S(2)}) async-start(), calls=%async_computation.5 | async-start | bytes 1064960 | tf_op jit(solution)/shard_map/all_gather | solution.py:109
  8.6 381.1 %all-gather.12.cloned.1.call-start = ((), (), s32[]{:S(2)}) async-start(), calls=%async_computation.3 | async-start | bytes 1064960 | tf_op jit(solution)/shard_map/all_gather | solution.py:110
  9.4 415.9 %all-gather.14.cloned.1.call-start = ((), (), s32[]{:S(2)}) async-start(), calls=%async_computation.4 | async-start | bytes 1064960 | tf_op jit(solution)/shard_map/all_gather | solution.py:108
  10.0 477.4 %all-gather.18.cloned.1.call-start = ((), (), s32[]{:S(2)}) async-start(), calls=%async_computation.6 | async-start | bytes 1064960 | tf_op jit(solution)/shard_map/all_gather | solution.py:140
  383.2 1.6 copy-start
  387.8 6.3 collective-permute-start.8
  391.6 6.3 collective-permute-start
  394.1 6.3 collective-permute-start.9
  397.9 6.3 collective-permute-start.1
  400.4 6.3 collective-permute-start.10
  402.4 126.9 %reduce-scatter.3.cloned.1.call-start = ((), (), s32[]{:S(2)}) async-start(), calls=%async_computation.7 | async-start | bytes 1179648 | tf_op jit(solution)/shard_map/reduce_scatter | solution.py:142
  404.1 6.3 collective-permute-start.2
  406.7 6.4 collective-permute-start.11
  410.4 6.5 collective-permute-start.3
  413.1 8.5 collective-permute-start.12
  416.9 10.1 %collective-permute-start.4 = (bf16[256,2,128]{0,2,1:T(8,128)(2,1)S(1)}, bf16[256,2,128]{0,2,1:T(8,128)(2,1)}, u32[]{:S(2)}, u32[]{:S(2)}) collective-permute-start(bf16[256,2,128]{0,2,1:T(8,128)(2,1)S(1)} %collective-permute-done.3), channel_id=1, source_target_pairs={{0,8},{8,16},{16,24},{24,32},{32,40},{40,48},{48,56},{56,64},{64,7... | collective-permute-start | bytes 393224 | tf_op jit(solution)/shard_map/ppermute | solution.py:30
  421.6 10.1 %collective-permute-start.13 = (bf16[256,2,128]{2,0,1:T(8,128)(2,1)}, bf16[256,2,128]{2,0,1:T(8,128)(2,1)}, u32[]{:S(2)}, u32[]{:S(2)}) collective-permute-start(bf16[256,2,128]{2,0,1:T(8,128)(2,1)} %collective-permute-done.12), channel_id=1, source_target_pairs={{0,8},{8,16},{16,24},{24,32},{32,40},{40,48},{48,56},{56,64},{64,7... | collective-permute-start | bytes 393224 | tf_op jit(solution)/shard_map/ppermute | solution.py:30
  427.0 8.6 collective-permute-start.5
  431.7 8.7 collective-permute-start.14
  435.7 8.7 collective-permute-start.6
  440.4 8.9 %collective-permute-start.15 = (bf16[256,2,128]{2,0,1:T(8,128)(2,1)S(1)}, bf16[256,2,128]{2,0,1:T(8,128)(2,1)S(1)}, u32[]{:S(2)}, u32[]{:S(2)}) collective-permute-start(bf16[256,2,128]{2,0,1:T(8,128)(2,1)S(1)} %collective-permute-done.14), channel_id=1, source_target_pairs={{0,8},{8,16},{16,24},{24,32},{32,40},{40,48},{48,56},{56,64},{64,7... | collective-permute-start | bytes 393224 | tf_op jit(solution)/shard_map/ppermute | solution.py:30
  444.4 8.1 collective-permute-start.7
  452.4 1.6 copy-start.7
  452.4 2.6 copy-start.5
  452.4 2.6 copy-start.6
  454.0 1.0 copy-start.8
  487.4 41.9 %copy-start.4 = (bf16[256,256]{1,0:T(8,128)(2,1)S(1)}, bf16[256,256]{1,0:T(8,128)(2,1)}, u32[]{:S(2)}) copy-start(bf16[256,256]{1,0:T(8,128)(2,1)} %param.12) | copy-start | bytes 393220
  490.1 83.1 %all-gather.20.cloned.1.call-start = ((), (), s32[]{:S(2)}) async-start(), calls=%async_computation.8 | async-start | bytes 1179648 | tf_op jit(solution)/shard_map/all_gather | solution.py:146
  530.9 127.7 %all-gather.22.cloned.1.call-start = ((), (), s32[]{:S(2)}) async-start(), calls=%async_computation.9 | async-start | bytes 2129920 | tf_op jit(solution)/shard_map/all_gather | solution.py:152
  531.7 210.9 %all-gather.24.cloned.1.call-start = ((), (), s32[]{:S(2)}) async-start(), calls=%async_computation.10 | async-start | bytes 2129920 | tf_op jit(solution)/shard_map/all_gather | solution.py:153
  532.4 294.0 %all-gather.26.cloned.1.call-start = ((), (), s32[]{:S(2)}) async-start(), calls=%async_computation.11 | async-start | bytes 2129920 | tf_op jit(solution)/shard_map/all_gather | solution.py:156
  533.0 337.3 %reduce-scatter.5.cloned.1.call-start = ((), (), s32[]{:S(2)}) async-start(), calls=%async_computation.12 | async-start | bytes 1179648 | tf_op jit(solution)/shard_map/reduce_scatter | solution.py:158
  573.2 1.5 copy-start.1
  660.9 170.2 %copy-start.9 = (s32[16]{0:T(128)S(1)}, s32[16]{0:T(128)}, u32[]{:S(2)}) copy-start(s32[16]{0:T(128)} %param.14) | copy-start | bytes 196
  831.3 39.0 %copy-start.2 = (bf16[256,256]{1,0:T(8,128)(2,1)S(1)}, bf16[256,256]{1,0:T(8,128)(2,1)}, u32[]{:S(2)}) copy-start(bf16[256,256]{1,0:T(8,128)(2,1)} %add_convert_fusion.1) | copy-start | bytes 393220
  832.7 39.2 %copy-start.3 = (bf16[2,16,16,256]{3,2,1,0:T(8,128)(2,1)}, bf16[2,16,16,256]{3,2,1,0:T(8,128)(2,1)S(1)}, u32[]{:S(2)}) copy-start(bf16[2,16,16,256]{3,2,1,0:T(8,128)(2,1)S(1)} %scatter_fusion) | copy-start | bytes 786436
Sparse Core Ops, SparseCore 0:
  10.0 46.6 all-gather.9
  60.1 81.1 all-gather.15
  144.6 79.8 all-gather.11
  227.7 79.7 all-gather.13
  402.5 84.8 all-gather.17
  490.2 38.9 reduce-scatter.2
  531.9 41.2 all-gather.19
  576.6 81.9 all-gather.21
  661.9 80.5 all-gather.23
  745.8 80.5 all-gather.25
  831.2 39.0 reduce-scatter.4
where the time goes:
time: 882 us; the launch traced here: 878 us
  waiting for transfers between devices  400 us (45%)
  loops' own time  212 us (24%)
  local copies, waits for them, and re-layouts  137 us (16%)
  starting transfers between devices  49.6 us (6%)
  blocking collectives  25.7 us (3%)
  matrix products  24.5 us (3%)
  between operations  15.8 us (2%)
  other arithmetic  13.9 us (2%)
    another operation x1, loops' own time, prefix(): return lax.fori_loop(0, count - 1, lap, running)  212 us
    dynamic_slice x189, local copies, waits for them, and re-layouts, lap(): longer = join(running, jax.tree.map(lambda part: part[position], pieces))  124 us
    all_gather x1, waiting for transfers between devices, per_device(): lax.all_gather(wd, 'wide', axis=1, tiled=True)  83.8 us
    all_gather x1, waiting for transfers between devices, per_device(): gate_proj = add_second(lax.all_gather(wg, 'wide', axis=0, tiled=True))  83.4 us
    all_gather x1, waiting for transfers between devices, per_device(): up_proj = add_second(lax.all_gather(wu, 'wide', axis=0, tiled=True))  81.6 us
    ppermute x16, starting transfers between devices, shifted(): lax.ppermute(value, axis, [(source, source + steps) for source in range(f...  49 us
    all_gather x1, waiting for transfers between devices, per_device(): whole_two = lax.all_gather(first_res, 'narrow', axis=1, tiled=True)  40 us
    reduce_scatter x1, waiting for transfers between devices, per_device(): lax.psum_scatter(attn_terms.astype(jnp.bfloat16), 'narrow', scatter_dimen...  39.1 us
  transfers between devices with their start and end apart: 27, of which 13 were waited for; matrix products, arithmetic and copies ran while one was open for 19% of the time, Pallas kernels for 0%

commit v1 on v0

--- a/solution.py
+++ b/solution.py
@@ -143,7 +143,9 @@
         attn_terms.astype(jnp.bfloat16), "narrow", scatter_dimension=1, tiled=True
     ).astype(jnp.float32)
     first_res = (hidden_in.astype(jnp.float32) + attn_sum).astype(jnp.bfloat16)
-    whole_two = lax.all_gather(first_res, "narrow", axis=1, tiled=True)
+    whole_two = jnp.concatenate(
+        lax.all_to_all(jnp.stack([first_res] * lax.axis_size("narrow")), "narrow", 0, 0), axis=1
+    )
     normed_two = norm_rows(whole_two)
 
     def add_second(piece):

time: 882 us -> 813 us (0.922)
  waiting for transfers between devices: 400 us -> 329 us
  blocking collectives: 25.7 us -> 54.6 us
  loops' own time: 212 us -> 193 us
    all_gather x1 -> x0, waiting for transfers between devices: 40 us -> none  [per_device(): whole_two = lax.all_gather(first_res, 'narrow', axis=1, tiled=True)]
    all_gather x1, waiting for transfers between devices: 83.4 us -> 54.2 us  [per_device(): gate_proj = add_second(lax.all_gather(wg, 'wide', axis=0, tiled=True))]
    all_to_all x0 -> x1, blocking collectives: none -> 28.9 us  [per_device(): lax.all_to_all(jnp.stack([first_res] * lax.axis_size('narrow')), 'narrow'...]
    another operation x1, loops' own time: 212 us -> 193 us  [prefix(): return lax.fori_loop(0, count - 1, lap, running)]
  transfers between devices with their start and end apart: 27 -> 26, of which waited for: 13 -> 12; matrix products, arithmetic and copies ran while one was open for 19% -> 19% of each run, Pallas kernels for 0% -> 0%
where the time goes in v1:
time: 813 us; the launch traced here: 809 us
  waiting for transfers between devices  329 us (40%)
  loops' own time  193 us (24%)
  local copies, waits for them, and re-layouts  130 us (16%)
  blocking collectives  54.6 us (7%)
  starting transfers between devices  49.3 us (6%)
  matrix products  24.2 us (3%)
  between operations  16.1 us (2%)
  other arithmetic  12.1 us (1%)
    another operation x1, loops' own time, prefix(): return lax.fori_loop(0, count - 1, lap, running)  193 us
    dynamic_slice x189, local copies, waits for them, and re-layouts, lap(): longer = join(running, jax.tree.map(lambda part: part[position], pieces))  117 us
    all_gather x1, waiting for transfers between devices, per_device(): lax.all_gather(wd, 'wide', axis=1, tiled=True)  84 us
    all_gather x1, waiting for transfers between devices, per_device(): up_proj = add_second(lax.all_gather(wu, 'wide', axis=0, tiled=True))  81.6 us
    all_gather x1, waiting for transfers between devices, per_device(): gate_proj = add_second(lax.all_gather(wg, 'wide', axis=0, tiled=True))  54.2 us
    ppermute x16, starting transfers between devices, shifted(): lax.ppermute(value, axis, [(source, source + steps) for source in range(f...  48.9 us
    reduce_scatter x1, waiting for transfers between devices, per_device(): lax.psum_scatter(down_terms.astype(jnp.bfloat16), 'narrow', scatter_dimen...  37.7 us
    reduce_scatter x1, waiting for transfers between devices, per_device(): lax.psum_scatter(attn_terms.astype(jnp.bfloat16), 'narrow', scatter_dimen...  37 us
  transfers between devices with their start and end apart: 26, of which 12 were waited for; matrix products, arithmetic and copies ran while one was open for 19% of the time, Pallas kernels for 0%

profile of v1, /device:TPU:2, one launch (start us, length us, event | category | flops | bytes accessed | tf_op | source)
XLA Modules:
  0.0 809.4 jit_solution(17367300782184038188)
XLA Ops:
  10.0 0.9 convert_reduce_fusion.2
  11.0 1.3 dynamic-slice
  12.2 1.9 fusion.41
  14.1 2.0 fusion.25
  18.0 1.3 dynamic-update-slice
  19.3 25.7 %all-reduce.3 = (s32[64]{0:T(128)S(1)}, s32[64]{0:T(128)S(1)}, s32[64]{0:T(128)S(1)}) all-reduce(s32[64]{0:T(128)S(1)} %dynamic-update-slice, s32[64]{0:T(128)S(1)} %get-tuple-element.159, s32[64]{0:T(128)S(1)} %dynamic-update-slice.2), channel_id=1, replica_groups=mesh['wide'=64,'narrow'=8] {'wide'}, use_global_device_ids=true, to_apply=%add | all-reduce | flops 192 | bytes 1536
  45.0 310.9 %while.15 = (s32[]{:T(128)}, s32[]{:T(128)}, s32[]{:T(128)}, s32[]{:T(128)}, s32[64]{0:T(128)S(1)}, /*index=5*/s32[64]{0:T(128)S(1)}, s32[64]{0:T(128)S(1)}, s32[]{:T(128)}, s32[]{:T(128)}, s32[1]{0:T(128)}) while((s32[]{:T(128)}, s32[]{:T(128)}, s32[]{:T(128)}, s32[]{:T(128)}, s32[64]{0:T(128)S(1)}, /*index=5*/s32[64]{0:T(128)S(1)}, ...), condition=%wide.region_5.6_spmd, body=%wide.region_4.5_spmd.sunk | while | flops 17 | bytes 279 | solution.py:24
  356.0 1.2 fusion.37
  357.8 1.5 convert_reduce_fusion
  360.2 1.7 fusion.46
  362.4 1.9 collective-permute-start.8
  364.4 1.7 convolution_convert_fusion.2
  366.1 2.5 collective-permute-start
  368.7 1.9 collective-permute-start.9
  370.6 1.8 collective-permute-done
  372.4 1.9 collective-permute-start.1
  375.0 1.9 collective-permute-start.10
  377.0 1.7 collective-permute-done.1
  378.7 1.9 collective-permute-start.2
  381.2 1.9 collective-permute-start.11
  383.2 1.8 collective-permute-done.2
  385.0 2.2 collective-permute-start.3
  387.6 3.3 collective-permute-start.12
  391.5 4.6 collective-permute-start.4
  396.1 3.6 collective-permute-start.13
  399.8 1.7 fusion.45
  401.6 4.6 collective-permute-start.5
  406.2 3.7 collective-permute-start.14
  410.2 4.7 collective-permute-start.6
  415.0 3.1 collective-permute-start.15
  418.9 5.0 collective-permute-start.7
  427.1 1.4 constant_dynamic-update-slice_fusion.5
  428.6 1.0 copy-done.6
  429.6 6.0 fusion.42
  435.6 3.3 fusion.13
  438.9 23.0 %all-gather.17.cloned.1.call-done = bf16[256,2048]{0,1:T(8,128)(2,1)} async-done(((bf16[256,32]{0,1:T(8,128)(2,1)}), bf16[256,2048]{0,1:T(8,128)(2,1)}) %all-gather.17.cloned.1.call-update) | async-done | bytes 1048592 | tf_op jit(solution)/shard_map/all_gather | solution.py:140
  461.9 2.8 convolution_convert_fusion.1
  467.0 37.0 %reduce-scatter.3.cloned.1.call-done = bf16[256,256]{1,0:T(8,128)(2,1)} async-done(((bf16[256,2048]{1,0:T(8,128)(2,1)}), bf16[256,256]{1,0:T(8,128)(2,1)}) %reduce-scatter.3.cloned.1.call-update) | async-done | bytes 131088 | tf_op jit(solution)/shard_map/reduce_scatter | solution.py:142
  504.0 0.9 add_convert_fusion.1
  505.1 28.9 %all_to_all.5 = bf16[8,256,256]{1,2,0:T(8,128)(2,1)S(1)} all-to-all(bf16[8,256,256]{1,2,0:T(8,128)(2,1)S(1)} %stack.4), channel_id=1, replica_groups=mesh['wide'=64,'narrow'=8] {'narrow'}, dimensions={0} | all-to-all | bytes 2097152 | tf_op jit(solution)/shard_map/all_to_all | solution.py:147
  534.9 54.2 %all-gather.19.cloned.1.call-done = bf16[2048,512]{1,0:T(8,128)(2,1)} async-done(((bf16[32,512]{1,0:T(8,128)(2,1)}), bf16[2048,512]{1,0:T(8,128)(2,1)}) %all-gather.19.cloned.1.call-update) | async-done | bytes 2097168 | tf_op jit(solution)/shard_map/all_gather | solution.py:154
  589.1 2.3 fusion.47
  591.4 81.6 %all-gather.21.cloned.1.call-done = bf16[2048,512]{1,0:T(8,128)(2,1)} async-done(((bf16[32,512]{1,0:T(8,128)(2,1)}), bf16[2048,512]{1,0:T(8,128)(2,1)}) %all-gather.21.cloned.1.call-update) | async-done | bytes 2097168 | tf_op jit(solution)/shard_map/all_gather | solution.py:155
  673.1 84.0 %all-gather.23.cloned.1.call-done = bf16[512,2048]{0,1:T(8,128)(2,1)} async-done(((bf16[512,32]{0,1:T(8,128)(2,1)}), bf16[512,2048]{0,1:T(8,128)(2,1)}) %all-gather.23.cloned.1.call-update) | async-done | bytes 2097168 | tf_op jit(solution)/shard_map/all_gather | solution.py:158
  757.1 4.6 convolution_convert_fusion
  762.1 1.2 scatter_fusion
  763.3 37.7 %reduce-scatter.5.cloned.1.call-done = bf16[256,256]{1,0:T(8,128)(2,1)} async-done(((bf16[256,2048]{1,0:T(8,128)(2,1)}), bf16[256,256]{1,0:T(8,128)(2,1)}) %reduce-scatter.5.cloned.1.call-update) | async-done | bytes 131088 | tf_op jit(solution)/shard_map/reduce_scatter | solution.py:160
  801.0 1.6 add_convert_fusion
  (296 shorter events, 133.1 us)
Async XLA Ops:
  7.2 350.6 %all-gather.9.cloned.1.call-start = ((), (), s32[]{:S(2)}) async-start(), calls=%async_computation.3 | async-start | bytes 1179648 | tf_op jit(solution)/shard_map/all_gather | solution.py:100
  7.9 352.3 %all-gather.15.cloned.1.call-start = ((), (), s32[]{:S(2)}) async-start(), calls=%async_computation.6 | async-start | bytes 1064960 | tf_op jit(solution)/shard_map/all_gather | solution.py:109
  8.6 355.7 %all-gather.11.cloned.1.call-start = ((), (), s32[]{:S(2)}) async-start(), calls=%async_computation.4 | async-start | bytes 1064960 | tf_op jit(solution)/shard_map/all_gather | solution.py:110
  9.4 390.4 %all-gather.13.cloned.1.call-start = ((), (), s32[]{:S(2)}) async-start(), calls=%async_computation.5 | async-start | bytes 1064960 | tf_op jit(solution)/shard_map/all_gather | solution.py:108
  10.0 451.9 %all-gather.17.cloned.1.call-start = ((), (), s32[]{:S(2)}) async-start(), calls=%async_computation.7 | async-start | bytes 1064960 | tf_op jit(solution)/shard_map/all_gather | solution.py:140
  357.8 1.6 copy-start
  362.4 6.3 collective-permute-start.8
  366.1 6.3 collective-permute-start
  368.7 6.3 collective-permute-start.9
  372.4 6.3 collective-permute-start.1
  375.0 6.3 collective-permute-start.10
  376.9 127.1 %reduce-scatter.3.cloned.1.call-start = ((), (), s32[]{:S(2)}) async-start(), calls=%async_computation.8 | async-start | bytes 1179648 | tf_op jit(solution)/shard_map/reduce_scatter | solution.py:142
  378.7 6.3 collective-permute-start.2
  381.2 6.4 collective-permute-start.11
  385.0 6.5 collective-permute-start.3
  387.6 8.5 %collective-permute-start.12 = (bf16[256,2,128]{2,0,1:T(8,128)(2,1)}, bf16[256,2,128]{2,0,1:T(8,128)(2,1)}, u32[]{:S(2)}, u32[]{:S(2)}) collective-permute-start(bf16[256,2,128]{2,0,1:T(8,128)(2,1)} %collective-permute-done.11), channel_id=1, source_target_pairs={{0,8},{8,16},{16,24},{24,32},{32,40},{40,48},{48,56},{56,64},{64,7... | collective-permute-start | bytes 393224 | tf_op jit(solution)/shard_map/ppermute | solution.py:30
  391.5 10.1 %collective-permute-start.4 = (bf16[256,2,128]{0,2,1:T(8,128)(2,1)S(1)}, bf16[256,2,128]{0,2,1:T(8,128)(2,1)}, u32[]{:S(2)}, u32[]{:S(2)}) collective-permute-start(bf16[256,2,128]{0,2,1:T(8,128)(2,1)S(1)} %collective-permute-done.3), channel_id=1, source_target_pairs={{0,8},{8,16},{16,24},{24,32},{32,40},{40,48},{48,56},{56,64},{64,7... | collective-permute-start | bytes 393224 | tf_op jit(solution)/shard_map/ppermute | solution.py:30
  396.1 10.1 %collective-permute-start.13 = (bf16[256,2,128]{2,0,1:T(8,128)(2,1)}, bf16[256,2,128]{2,0,1:T(8,128)(2,1)}, u32[]{:S(2)}, u32[]{:S(2)}) collective-permute-start(bf16[256,2,128]{2,0,1:T(8,128)(2,1)} %collective-permute-done.12), channel_id=1, source_target_pairs={{0,8},{8,16},{16,24},{24,32},{32,40},{40,48},{48,56},{56,64},{64,7... | collective-permute-start | bytes 393224 | tf_op jit(solution)/shard_map/ppermute | solution.py:30
  401.6 8.6 %collective-permute-start.5 = (bf16[256,2,128]{0,2,1:T(8,128)(2,1)}, bf16[256,2,128]{0,2,1:T(8,128)(2,1)S(1)}, u32[]{:S(2)}, u32[]{:S(2)}) collective-permute-start(bf16[256,2,128]{0,2,1:T(8,128)(2,1)} %collective-permute-done.4), channel_id=1, source_target_pairs={{0,8},{8,16},{16,24},{24,32},{32,40},{40,48},{48,56},{56,64},{64,7... | collective-permute-start | bytes 393224 | tf_op jit(solution)/shard_map/ppermute | solution.py:30
  406.2 8.7 %collective-permute-start.14 = (bf16[256,2,128]{2,0,1:T(8,128)(2,1)}, bf16[256,2,128]{2,0,1:T(8,128)(2,1)S(1)}, u32[]{:S(2)}, u32[]{:S(2)}) collective-permute-start(bf16[256,2,128]{2,0,1:T(8,128)(2,1)} %collective-permute-done.13), channel_id=1, source_target_pairs={{0,8},{8,16},{16,24},{24,32},{32,40},{40,48},{48,56},{56,64},{64,7... | collective-permute-start | bytes 393224 | tf_op jit(solution)/shard_map/ppermute | solution.py:30
  410.2 8.7 %collective-permute-start.6 = (bf16[256,2,128]{0,2,1:T(8,128)(2,1)S(1)}, bf16[256,2,128]{0,2,1:T(8,128)(2,1)S(1)}, u32[]{:S(2)}, u32[]{:S(2)}) collective-permute-start(bf16[256,2,128]{0,2,1:T(8,128)(2,1)S(1)} %collective-permute-done.5), channel_id=1, source_target_pairs={{0,8},{8,16},{16,24},{24,32},{32,40},{40,48},{48,56},{56,64},{64,7... | collective-permute-start | bytes 393224 | tf_op jit(solution)/shard_map/ppermute | solution.py:30
  415.0 8.9 %collective-permute-start.15 = (bf16[256,2,128]{2,0,1:T(8,128)(2,1)S(1)}, bf16[256,2,128]{2,0,1:T(8,128)(2,1)S(1)}, u32[]{:S(2)}, u32[]{:S(2)}) collective-permute-start(bf16[256,2,128]{2,0,1:T(8,128)(2,1)S(1)} %collective-permute-done.14), channel_id=1, source_target_pairs={{0,8},{8,16},{16,24},{24,32},{32,40},{40,48},{48,56},{56,64},{64,7... | collective-permute-start | bytes 393224 | tf_op jit(solution)/shard_map/ppermute | solution.py:30
  418.9 8.1 %collective-permute-start.7 = (bf16[256,2,128]{0,2,1:T(8,128)(2,1)S(1)}, bf16[256,2,128]{0,2,1:T(8,128)(2,1)S(1)}, u32[]{:S(2)}, u32[]{:S(2)}) collective-permute-start(bf16[256,2,128]{0,2,1:T(8,128)(2,1)S(1)} %collective-permute-done.6), channel_id=1, source_target_pairs={{0,8},{8,16},{16,24},{24,32},{32,40},{40,48},{48,56},{56,64},{64,7... | collective-permute-start | bytes 393224 | tf_op jit(solution)/shard_map/ppermute | solution.py:30
  427.0 1.6 copy-start.5
  427.0 2.6 copy-start.3
  427.0 2.6 copy-start.4
  428.5 1.1 copy-start.6
  429.6 6.0 copy-start.7
  461.9 42.1 %copy-start.2 = (bf16[256,256]{1,0:T(8,128)(2,1)S(1)}, bf16[256,256]{1,0:T(8,128)(2,1)}, u32[]{:S(2)}) copy-start(bf16[256,256]{1,0:T(8,128)(2,1)} %param.12) | copy-start | bytes 393220
  464.7 124.4 %all-gather.19.cloned.1.call-start = ((), (), s32[]{:S(2)}) async-start(), calls=%async_computation.9 | async-start | bytes 2129920 | tf_op jit(solution)/shard_map/all_gather | solution.py:154
  465.5 207.6 %all-gather.21.cloned.1.call-start = ((), (), s32[]{:S(2)}) async-start(), calls=%async_computation.10 | async-start | bytes 2129920 | tf_op jit(solution)/shard_map/all_gather | solution.py:155
  466.2 290.9 %all-gather.23.cloned.1.call-start = ((), (), s32[]{:S(2)}) async-start(), calls=%async_computation.11 | async-start | bytes 2129920 | tf_op jit(solution)/shard_map/all_gather | solution.py:158
  467.0 334.0 %reduce-scatter.5.cloned.1.call-start = ((), (), s32[]{:S(2)}) async-start(), calls=%async_computation.12 | async-start | bytes 1179648 | tf_op jit(solution)/shard_map/reduce_scatter | solution.py:160
  591.4 170.3 %copy-start.8 = (s32[16]{0:T(128)S(1)}, s32[16]{0:T(128)}, u32[]{:S(2)}) copy-start(s32[16]{0:T(128)} %param.14) | copy-start | bytes 196
  763.3 39.3 %copy-start.1 = (bf16[2,16,16,256]{3,2,1,0:T(8,128)(2,1)}, bf16[2,16,16,256]{3,2,1,0:T(8,128)(2,1)S(1)}, u32[]{:S(2)}) copy-start(bf16[2,16,16,256]{3,2,1,0:T(8,128)(2,1)S(1)} %scatter_fusion) | copy-start | bytes 786436
Sparse Core Ops, SparseCore 0:
  10.0 46.6 all-gather.8
  60.1 81.1 all-gather.14
  144.6 79.8 all-gather.10
  227.7 79.7 all-gather.12
  377.0 84.8 all-gather.16
  464.8 39.1 reduce-scatter.2
  507.3 81.7 all-gather.18
  592.5 80.5 all-gather.20
  676.5 80.5 all-gather.22
  761.8 39.0 reduce-scatter.4
